TPU v7x, 32 devices: a whole 2x2x4 slice. The times are simulated.
32 devices in a mesh: dp: 4 (over z), expert: 8 (over y, x, core).
Axes of the slice: x: 2, y: 2, z: 4, core: 2. Of those that a mesh axis runs over, the one named last changes fastest.
Arguments:
- tokens: bfloat16 [384, 4096], P('expert', 'dp'), may hold values from -6 to 6
- out_grad: bfloat16 [384, 4096], P('expert', 'dp'), may hold values from -6 to 6
- expert_ids: int32 [384, 8], P('expert'), may hold values from 0 to 63, all different within a row; in each aligned block of 48 rows (0 to 47, 48 to 95, ...) at most 12 rows name the same one
- route_weights: float32 [384, 8], P('expert'), may hold values from 0.05 to 1
- gate_weight: bfloat16 [64, 4096, 768], P('expert', 'dp'), may hold values from -0.09375 to 0.09375
- up_weight: bfloat16 [64, 4096, 768], P('expert', 'dp'), may hold values from -0.09375 to 0.09375
- down_weight: bfloat16 [64, 768, 4096], P('expert', None, 'dp'), may hold values from -0.21875 to 0.21875
Outputs:
- layer_out: bfloat16 [384, 4096], P('expert', 'dp')
- grad_tokens: bfloat16 [384, 4096], P('expert', 'dp')
- gate_grad: bfloat16 [64, 4096, 768], P('expert', 'dp')
- up_grad: bfloat16 [64, 4096, 768], P('expert', 'dp')
- down_grad: bfloat16 [64, 768, 4096], P('expert', None, 'dp')
Inputs may be any that keep to these rules, and one draw needn't show every extreme that they name: `expert_ids`: each row names 8 different experts. In the 48 rows of one index of the expert axis no expert is named more than 12 times, and in every draw some expert is named exactly 12 times there.
All inputs are finite; a program needn't handle non-finite values.
Results may differ from a plain program's by a relative error of at most 0.029.
Values may be sent and summed in bfloat16 or wider, within the bound.
No kernel may reach another device: no remote copies, remote signals or barrier semaphores. Data moves between devices by JAX's collectives and lax.ppermute only.
A program may use at most 128 MiB of HBM per device.

v0:
```python
import jax
import jax.numpy as jnp
from jax import lax
from jax.sharding import PartitionSpec as P


def swiglu_parts(gate_sum, up_sum, back_sum):
    logistic = jax.nn.sigmoid(gate_sum)
    activated = gate_sum * logistic
    hidden = (activated * up_sum).astype(jnp.bfloat16)
    gate_delta = (back_sum * up_sum * logistic * (1.0 + gate_sum * (1.0 - logistic))).astype(
        jnp.bfloat16
    )
    up_delta = (back_sum * activated).astype(jnp.bfloat16)
    return (hidden, gate_delta, up_delta)


def split_f32(value):
    high = value.astype(jnp.bfloat16)
    rest = value - high.astype(jnp.float32)
    middle = rest.astype(jnp.bfloat16)
    low = (rest - middle.astype(jnp.float32)).astype(jnp.bfloat16)
    return high, middle, low


def local(tokens, out_grad, expert_ids, route_weights, gate_weight, up_weight, down_weight):
    token_count, width_dev = tokens.shape
    per_token = expert_ids.shape[1]
    local_experts = gate_weight.shape[0]
    hidden_units = gate_weight.shape[2]
    sources = lax.axis_size("expert")
    experts = local_experts * sources
    capacity = 2 * token_count * per_token // experts
    slot_count = token_count * per_token
    me = lax.axis_index("expert")

    high, middle, low = split_f32(route_weights)
    route_cols = 4 * per_token
    pad_cols = (-route_cols) % 128
    packed = jnp.concatenate(
        [
            tokens,
            out_grad,
            expert_ids.astype(jnp.bfloat16),
            high,
            middle,
            low,
            jnp.zeros((token_count, pad_cols), jnp.bfloat16),
        ],
        axis=1,
    )
    gathered = lax.all_gather(packed, "expert", axis=0, tiled=True)
    feats = gathered[:, : 2 * width_dev]
    route_all = gathered[:, 2 * width_dev : 2 * width_dev + route_cols].astype(jnp.float32)
    ids_all = route_all[:, :per_token].astype(jnp.int32)
    w_all = (
        route_all[:, per_token : 2 * per_token] + route_all[:, 2 * per_token : 3 * per_token]
    ) + route_all[:, 3 * per_token :]
    all_tokens = sources * token_count

    flat_all = ids_all.reshape(sources, slot_count)
    position = jnp.arange(slot_count, dtype=jnp.int32)
    earlier = (flat_all[:, None, :] == flat_all[:, :, None]) & (
        position[None, None, :] < position[None, :, None]
    )
    rank_all = jnp.sum(earlier.astype(jnp.int32), axis=2)
    local_e = flat_all - me * local_experts
    is_local = (local_e >= 0) & (local_e < local_experts)
    src = jnp.arange(sources, dtype=jnp.int32)[:, None]
    row_count = local_experts * sources * capacity
    row_of = jnp.where(is_local, (local_e * sources + src) * capacity + rank_all, row_count)
    row_of = row_of.reshape(sources * slot_count)
    token_of = jnp.arange(sources * slot_count, dtype=jnp.int32) // per_token
    target = jnp.arange(row_count, dtype=jnp.int32)
    hit = target[:, None] == row_of[None, :]
    holder = jnp.sum(jnp.where(hit, token_of[None, :] + 1, 0), axis=1) - 1
    row_weight = jnp.sum(jnp.where(hit, w_all.reshape(-1)[None, :], 0.0), axis=1)
    select = (holder[:, None] == jnp.arange(all_tokens, dtype=jnp.int32)[None, :]).astype(
        jnp.bfloat16
    )
    picked = jnp.dot(select, feats, preferred_element_type=jnp.float32)
    x_in = picked[:, :width_dev].astype(jnp.bfloat16)
    dy_in = (row_weight[:, None] * picked[:, width_dev:]).astype(jnp.bfloat16)
    x_in = x_in.reshape(local_experts, sources * capacity, width_dev)
    dy_in = dy_in.reshape(local_experts, sources * capacity, width_dev)

    gate_part = jnp.einsum(
        "jrd,jdf->jrf", x_in, gate_weight, preferred_element_type=jnp.float32
    ).astype(jnp.bfloat16)
    up_part = jnp.einsum(
        "jrd,jdf->jrf", x_in, up_weight, preferred_element_type=jnp.float32
    ).astype(jnp.bfloat16)
    front = jnp.concatenate([gate_part, up_part], axis=2).reshape(row_count, 2 * hidden_units)
    front_sums = lax.psum_scatter(front, "dp", scatter_dimension=0, tiled=True)
    back_part = jnp.einsum(
        "jrd,jfd->jrf", dy_in, down_weight, preferred_element_type=jnp.float32
    ).astype(jnp.bfloat16)
    back_sums = lax.psum_scatter(
        back_part.reshape(row_count, hidden_units), "dp", scatter_dimension=0, tiled=True
    )
    front_sums = front_sums.astype(jnp.float32)
    hidden, gate_delta, up_delta = swiglu_parts(
        front_sums[:, :hidden_units], front_sums[:, hidden_units:], back_sums.astype(jnp.float32)
    )
    first = lax.all_gather(
        jnp.concatenate([hidden, gate_delta], axis=1), "dp", axis=0, tiled=True
    )
    up_delta, first = lax.optimization_barrier((up_delta, first))
    up_delta = lax.all_gather(up_delta, "dp", axis=0, tiled=True)
    rows_shape = (local_experts, sources * capacity, hidden_units)
    expert_shape = (local_experts, sources, capacity, hidden_units)
    hidden = first[:, :hidden_units]
    gate_delta = first[:, hidden_units:]

    buffer_rows = experts * capacity
    expert_out = jnp.einsum(
        "jscf,jfd->sjcd", hidden.reshape(expert_shape), down_weight,
        preferred_element_type=jnp.float32,
    ).astype(jnp.bfloat16)
    out_back = lax.all_to_all(
        expert_out.reshape(buffer_rows, width_dev), "expert", split_axis=0, concat_axis=0, tiled=True
    )
    down_grad = jnp.einsum(
        "jrf,jrd->jfd", hidden.reshape(rows_shape), dy_in, preferred_element_type=jnp.float32
    ).astype(jnp.bfloat16)
    gate_back = jnp.einsum(
        "jscf,jdf->sjcd", gate_delta.reshape(expert_shape), gate_weight,
        preferred_element_type=jnp.float32,
    )
    gate_grad = jnp.einsum(
        "jrd,jrf->jdf", x_in, gate_delta.reshape(rows_shape), preferred_element_type=jnp.float32
    ).astype(jnp.bfloat16)
    expert_back = (
        gate_back
        + jnp.einsum(
            "jscf,jdf->sjcd", up_delta.reshape(expert_shape), up_weight,
            preferred_element_type=jnp.float32,
        )
    ).astype(jnp.bfloat16)
    grad_back = lax.all_to_all(
        expert_back.reshape(buffer_rows, width_dev), "expert", split_axis=0, concat_axis=0, tiled=True
    )
    up_grad = jnp.einsum(
        "jrd,jrf->jdf", x_in, up_delta.reshape(rows_shape), preferred_element_type=jnp.float32
    ).astype(jnp.bfloat16)

    flat_ids = expert_ids.reshape(slot_count)
    earlier_local = (flat_ids[None, :] == flat_ids[:, None]) & (
        position[None, :] < position[:, None]
    )
    slot_rank = jnp.sum(earlier_local.astype(jnp.int32), axis=1)
    slot_place = (flat_ids * capacity + slot_rank).reshape(token_count, per_token)
    picked_out = jnp.take(out_back, slot_place, axis=0).astype(jnp.float32)
    layer_out = jnp.sum(picked_out * route_weights[:, :, None], axis=1).astype(jnp.bfloat16)
    picked_back = jnp.take(grad_back, slot_place, axis=0).astype(jnp.float32)
    grad_tokens = jnp.sum(picked_back, axis=1).astype(jnp.bfloat16)
    return (layer_out, grad_tokens, gate_grad, up_grad, down_grad)


def solution(mesh):
    in_specs = (
        P("expert", "dp"),
        P("expert", "dp"),
        P("expert", None),
        P("expert", None),
        P("expert", "dp", None),
        P("expert", "dp", None),
        P("expert", None, "dp"),
    )
    out_specs = (
        P("expert", "dp"),
        P("expert", "dp"),
        P("expert", "dp", None),
        P("expert", "dp", None),
        P("expert", None, "dp"),
    )
    return jax.shard_map(local, mesh=mesh, in_specs=in_specs, out_specs=out_specs, check_vma=False)
```

profile of v0, /device:TPU:0, one launch (start us, length us, event | category | flops | bytes accessed | tf_op | source)
XLA Modules:
  0.0 287.8 jit_solution(4165284940763575105)
XLA Ops:
  9.1 1.7 concatenate.9
  10.9 28.8 %all-gather.4.cloned.1.call-done = bf16[384,2176]{1,0:T(8,128)(2,1)} async-done(((bf16[48,2176]{1,0:T(8,128)(2,1)}), bf16[384,2176]{1,0:T(8,128)(2,1)}) %all-gather.4.cloned.1.call-update) | async-done | bytes 1671184 | tf_op jit(solution)/shard_map/all_gather | solution.py:52
  41.5 1.6 convert_reduce_fusion
  44.5 1.8 fusion.12
  46.3 3.2 %copy-done.3 = f32[768,2048]{1,0:T(8,128)} copy-done((f32[768,2048]{1,0:T(8,128)}, f32[768,2048]{1,0:T(8,128)S(1)}, u32[]{:S(2)}) %copy-start.3) | copy-done | bytes 6291480
  49.8 2.1 copy-done
  51.8 2.0 convolution_convert_fusion.3
  55.7 2.0 convolution_convert_fusion.4
  60.8 2.1 fusion.6
  63.0 10.0 %convolution_convert_fusion.5 = bf16[8,96,768]{2,1,0:T(8,128)(2,1)} fusion(bf16[8,96,1024]{2,1,0:T(8,128)(2,1)S(1)} %bitcast.64, bf16[8,768,1024]{2,1,0:T(8,128)(2,1)} %param.15), kind=kOutput, calls=%fused_computation.27 | convolution fusion | flops 1208549376 | bytes 15335424 | tf_op jit(solution)/shard_map/jrd,jfd->jrf/dot_general | solution.py:95
  73.0 34.4 %reduce-scatter.5.cloned.1.call-done = bf16[192,1536]{1,0:T(8,128)(2,1)} async-done(((bf16[768,1536]{1,0:T(8,128)(2,1)}), bf16[192,1536]{1,0:T(8,128)(2,1)}) %reduce-scatter.5.cloned.1.call-update) | async-done | bytes 589840 | tf_op jit(solution)/shard_map/reduce_scatter | solution.py:94
  108.7 30.4 %reduce-scatter.3.cloned.1.call-done = bf16[192,768]{1,0:T(8,128)(2,1)} async-done(((bf16[768,768]{1,0:T(8,128)(2,1)}), bf16[192,768]{1,0:T(8,128)(2,1)}) %reduce-scatter.3.cloned.1.call-update) | async-done | bytes 294928 | tf_op jit(solution)/shard_map/reduce_scatter | solution.py:98
  139.1 2.0 fusion.18
  143.0 48.3 %all-gather.6.cloned.1.call-done = bf16[768,1536]{1,0:T(8,128)(2,1)} async-done(((bf16[192,1536]{1,0:T(8,128)(2,1)}), bf16[768,1536]{1,0:T(8,128)(2,1)}) %all-gather.6.cloned.1.call-update) | async-done | bytes 2359312 | tf_op jit(solution)/shard_map/all_gather | solution.py:105
  191.3 2.8 fusion.26
  195.6 3.1 %reshape.133 = bf16[8,8,12,768]{3,2,1,0:T(8,128)(2,1)} reshape(bf16[768,768]{1,0:T(8,128)(2,1)} %get-tuple-element.13) | data formatting | bytes 2359296 | tf_op jit(solution)/shard_map/reshape | solution.py:117
  198.8 7.1 %convert_bitcast_fusion = bf16[8,8,12,1024]{3,2,0,1:T(8,128)(2,1)S(1)} fusion(bf16[8,8,12,768]{3,2,1,0:T(8,128)(2,1)} %reshape.133, bf16[8,768,1024]{2,1,0:T(8,128)(2,1)} %param.15), kind=kOutput, calls=%fused_computation.21 | convolution fusion | flops 1208745984 | bytes 15335424 | tf_op jit(solution)/shard_map/jscf,jfd->sjcd/dot_general | solution.py:116
  206.8 2.0 copy.63
  208.8 4.7 %all-to-all-start = ((bf16[8,96,1024]{2,1,0:T(8,128)(2,1)}), bf16[8,96,1024]{2,1,0:T(8,128)(2,1)}, u32[]{:S(2)}, u32[]{:S(2)}) async-start(bf16[8,96,1024]{2,1,0:T(8,128)(2,1)} %copy.63), calls=%async_computation.2 | async-start | bytes 3145728 | tf_op jit(solution)/shard_map/all_to_all | solution.py:120
  213.5 6.6 %convolution_convert_fusion = bf16[8,768,1024]{2,1,0:T(8,128)(2,1)} fusion(bf16[8,96,768]{2,1,0:T(8,128)(2,1)S(1)} %bitcast.67, bf16[8,96,1024]{2,1,0:T(8,128)(2,1)S(1)} %bitcast.65), kind=kOutput, calls=%fused_computation.11 | convolution fusion | flops 1214251008 | bytes 15335424 | tf_op jit(solution)/shard_map/jrf,jrd->jfd/dot_general | solution.py:123
  220.1 3.4 %all-gather.8.cloned.1.call-done = bf16[768,768]{1,0:T(8,128)(2,1)} async-done(((bf16[192,768]{1,0:T(8,128)(2,1)}), bf16[768,768]{1,0:T(8,128)(2,1)}) %all-gather.8.cloned.1.call-update) | async-done | bytes 1179664 | tf_op jit(solution)/shard_map/all_gather | solution.py:109
  223.6 3.1 %reshape.135 = bf16[8,8,12,768]{3,2,1,0:T(8,128)(2,1)} reshape(bf16[768,768]{1,0:T(8,128)(2,1)} %all-gather.8.cloned.1.call-done) | data formatting | bytes 2359296 | tf_op jit(solution)/shard_map/reshape | solution.py:136
  226.7 9.1 %fusion = f32[8,8,12,1024]{3,2,1,0:T(8,128)S(1)} fusion(bf16[8,8,12,768]{3,2,1,0:T(8,128)(2,1)} %reshape.135, bf16[8,1024,768]{2,1,0:T(8,128)(2,1)} %param.14), kind=kOutput, calls=%fused_computation.2 | convolution fusion | flops 1207959552 | bytes 16908288 | tf_op jit(solution)/shard_map/jscf,jdf->sjcd/dot_general | solution.py:135
  235.8 10.6 %fusion.7 = bf16[8,8,12,1024]{3,2,0,1:T(8,128)(2,1)} fusion(f32[8,8,12,1024]{3,2,1,0:T(8,128)S(1)} %fusion, bf16[8,8,12,768]{3,2,1,0:T(8,128)(2,1)} %reshape.134, bf16[8,1024,768]{2,1,0:T(8,128)(2,1)} %param.13), kind=kOutput, calls=%fused_computation.20 | convolution fusion | flops 1209532416 | bytes 18481152 | tf_op jit(solution)/shard_map/jscf,jdf->sjcd/dot_general | solution.py:126
  246.4 2.5 copy.67
  248.9 2.0 copy.68
  250.9 4.0 %all-to-all-start.1 = ((bf16[8,96,1024]{2,1,0:T(8,128)(2,1)}), bf16[8,96,1024]{2,1,0:T(8,128)(2,1)S(1)}, u32[]{:S(2)}, u32[]{:S(2)}) async-start(bf16[8,96,1024]{2,1,0:T(8,128)(2,1)} %copy.68), calls=%async_computation.3 | async-start | bytes 3145728 | tf_op jit(solution)/shard_map/all_to_all | solution.py:140
  254.9 7.9 %convolution_convert_fusion.2 = bf16[8,1024,768]{2,1,0:T(8,128)(2,1)} fusion(bf16[8,96,1024]{2,1,0:T(8,128)(2,1)S(1)} %bitcast.61, bf16[8,96,768]{2,1,0:T(8,128)(2,1)} %bitcast.66), kind=kOutput, calls=%fused_computation.13 | convolution fusion | flops 1214251008 | bytes 15335424 | tf_op jit(solution)/shard_map/jrd,jrf->jdf/dot_general | solution.py:130
  262.8 5.0 %gather_fusion = bf16[384,1024]{1,0:T(8,128)(2,1)} fusion(bf16[768,1024]{1,0:T(8,128)(2,1)} %bitcast.8, s32[1024]{0:T(1024)S(1)} %pad_clamp_fusion), kind=kCustom, calls=%fused_computation.clone | custom fusion | bytes 1574400 | tf_op jit(solution)/shard_map/jit(_take)/gather | solution.py:153
  267.8 2.4 multiply_reduce_fusion
  270.2 7.9 %convolution_convert_fusion.1 = bf16[8,1024,768]{2,1,0:T(8,128)(2,1)} fusion(bf16[8,96,1024]{2,1,0:T(8,128)(2,1)S(1)} %bitcast.62, bf16[8,96,768]{2,1,0:T(8,128)(2,1)} %bitcast.72), kind=kOutput, calls=%fused_computation.12 | convolution fusion | flops 1214251008 | bytes 15335424 | tf_op jit(solution)/shard_map/jrd,jrf->jdf/dot_general | solution.py:143
  278.1 2.1 gather_fusion.1
  (76 shorter events, 16.8 us)
Async XLA Ops:
  7.2 32.6 %all-gather.4.cloned.1.call-start = ((), (), s32[]{:S(2)}) async-start(), calls=%async_computation.4 | async-start | bytes 1880064 | tf_op jit(solution)/shard_map/all_gather | solution.py:52
  10.8 96.6 %reduce-scatter.5.cloned.1.call-start = ((), (), s32[]{:S(2)}) async-start(), calls=%async_computation.6 | async-start | bytes 2949120 | tf_op jit(solution)/shard_map/reduce_scatter | solution.py:94
  39.8 4.7 %copy-start.6 = (bf16[384,2176]{1,0:T(8,128)(2,1)S(1)}, bf16[384,2176]{1,0:T(8,128)(2,1)}, u32[]{:S(2)}) copy-start(bf16[384,2176]{1,0:T(8,128)(2,1)} %all-gather.4.cloned.1.call-done) | copy-start | bytes 5013508
  44.4 7.4 %copy-start = (bf16[8,1024,768]{2,1,0:T(8,128)(2,1)S(1)}, bf16[8,1024,768]{2,1,0:T(8,128)(2,1)}, u32[]{:S(2)}) copy-start(bf16[8,1024,768]{2,1,0:T(8,128)(2,1)} %param.14) | copy-start | bytes 37748740
  44.4 9.4 %slice-start = ((s8[12582912]{0:T(1024)(128)(4,1)}), s8[4194304]{0:T(1024)(128)(4,1)S(1)}, s32[]{:S(2)}) async-start(s8[12582912]{0:T(1024)(128)(4,1)} %bitcast.57), calls=%async_computation.9 | async-start | bytes 8388608
  44.5 9.8 %slice-start.1 = ((s8[12582912]{0:T(1024)(128)(4,1)}), s8[4194304]{0:T(1024)(128)(4,1)S(1)}, s32[]{:S(2)}) async-start(s8[12582912]{0:T(1024)(128)(4,1)} %bitcast.57), calls=%async_computation.10 | async-start | bytes 8388608
  46.3 3.2 %copy-start.3 = (f32[768,2048]{1,0:T(8,128)}, f32[768,2048]{1,0:T(8,128)S(1)}, u32[]{:S(2)}) copy-start(f32[768,2048]{1,0:T(8,128)S(1)} %fusion.12) | copy-start | bytes 18874372
  49.8 4.1 %copy-start.1 = (bf16[768,1024]{1,0:T(8,128)(2,1)}, bf16[768,1024]{1,0:T(8,128)(2,1)S(1)}, u32[]{:S(2)}) copy-start(bf16[768,1024]{1,0:T(8,128)(2,1)S(1)} %slice.88) | copy-start | bytes 4718596
  51.8 3.8 %slice-start.2 = ((s8[12582912]{0:T(1024)(128)(4,1)}), s8[4194304]{0:T(1024)(128)(4,1)S(1)}, s32[]{:S(2)}) async-start(s8[12582912]{0:T(1024)(128)(4,1)} %bitcast.57), calls=%async_computation.11 | async-start | bytes 8388608
  59.3 79.8 %reduce-scatter.3.cloned.1.call-start = ((), (), s32[]{:S(2)}) async-start(), calls=%async_computation.5 | async-start | bytes 1474560 | tf_op jit(solution)/shard_map/reduce_scatter | solution.py:98
  73.0 118.3 %all-gather.6.cloned.1.call-start = ((), (), s32[]{:S(2)}) async-start(), calls=%async_computation.7 | async-start | bytes 2949120 | tf_op jit(solution)/shard_map/all_gather | solution.py:105
  108.6 33.4 %copy-start.8 = (f32[48,8]{0,1:T(8,128)S(1)}, f32[48,8]{0,1:T(8,128)}, u32[]{:S(2)}) copy-start(f32[48,8]{0,1:T(8,128)} %param.12) | copy-start | bytes 4612
  108.7 33.5 %copy-start.7 = (s32[48,8]{0,1:T(8,128)S(1)}, s32[48,8]{0,1:T(8,128)}, u32[]{:S(2)}) copy-start(s32[48,8]{0,1:T(8,128)} %param.11) | copy-start | bytes 4612
  142.0 81.6 %all-gather.8.cloned.1.call-start = ((), (), s32[]{:S(2)}) async-start(), calls=%async_computation.8 | async-start | bytes 1474560 | tf_op jit(solution)/shard_map/all_gather | solution.py:109
  194.1 4.6 %copy-start.4 = (bf16[768,768]{1,0:T(8,128)(2,1)}, bf16[768,768]{1,0:T(8,128)(2,1)S(1)}, u32[]{:S(2)}) copy-start(bf16[768,768]{1,0:T(8,128)(2,1)S(1)} %get-tuple-element.12) | copy-start | bytes 3538948
  208.8 4.7 %copy-start.5 = (bf16[768,768]{1,0:T(8,128)(2,1)S(1)}, bf16[768,768]{1,0:T(8,128)(2,1)}, u32[]{:S(2)}) copy-start(bf16[768,768]{1,0:T(8,128)(2,1)} %get-tuple-element.13) | copy-start | bytes 3538948
  208.8 42.1 %all-to-all-start = ((bf16[8,96,1024]{2,1,0:T(8,128)(2,1)}), bf16[8,96,1024]{2,1,0:T(8,128)(2,1)}, u32[]{:S(2)}, u32[]{:S(2)}) async-start(bf16[8,96,1024]{2,1,0:T(8,128)(2,1)} %copy.63), calls=%async_computation.2 | async-start | bytes 3145728 | tf_op jit(solution)/shard_map/all_to_all | solution.py:120
  250.9 4.0 %copy-start.2 = (bf16[768,1024]{1,0:T(8,128)(2,1)S(1)}, bf16[768,1024]{1,0:T(8,128)(2,1)}, u32[]{:S(2)}) copy-start(bf16[768,1024]{1,0:T(8,128)(2,1)} %copy-done.1) | copy-start | bytes 4718596
  250.9 27.2 %all-to-all-start.1 = ((bf16[8,96,1024]{2,1,0:T(8,128)(2,1)}), bf16[8,96,1024]{2,1,0:T(8,128)(2,1)S(1)}, u32[]{:S(2)}, u32[]{:S(2)}) async-start(bf16[8,96,1024]{2,1,0:T(8,128)(2,1)} %copy.68), calls=%async_computation.3 | async-start | bytes 3145728 | tf_op jit(solution)/shard_map/all_to_all | solution.py:140
Sparse Core Ops, SparseCore 0:
  10.9 28.7 all-gather.3
  59.4 48.0 reduce-scatter.4
  110.3 28.6 reduce-scatter.2
  142.1 49.1 all-gather.5
  194.3 29.2 all-gather.7
where the time goes:
time: 289 us; the launch traced here: 288 us
  waiting for transfers between devices  145 us (50%)
  matrix products  65.1 us (23%)
  local copies, waits for them, and re-layouts  35.7 us (12%)
  other arithmetic  18.4 us (6%)
  between operations  14.1 us (5%)
  starting transfers between devices  9.01 us (3%)
    all_gather x1, waiting for transfers between devices, local(): lax.all_gather(jnp.concatenate([hidden, gate_delta], axis=1), 'dp', axis=...  48.3 us
    reduce_scatter x1, waiting for transfers between devices, local(): front_sums = lax.psum_scatter(front, 'dp', scatter_dimension=0, tiled=True)  34.4 us
    reduce_scatter x1, waiting for transfers between devices, local(): lax.psum_scatter(back_part.reshape(row_count, hidden_units), 'dp', scatte...  30.4 us
    all_gather x1, waiting for transfers between devices, local(): gathered = lax.all_gather(packed, 'expert', axis=0, tiled=True)  28.8 us
    dot_general x1, matrix products, local(): jnp.einsum('jscf,jdf->sjcd', gate_delta.reshape(expert_shape), gate_weigh...  10.6 us
    dot_general x1, matrix products, local(): jnp.einsum('jrd,jfd->jrf', dy_in, down_weight, preferred_element_type=jnp...  10 us
    dot_general x1, matrix products, local(): jnp.einsum('jscf,jdf->sjcd', up_delta.reshape(expert_shape), up_weight, p...  9.12 us
    dot_general x1, matrix products, local(): jnp.einsum('jrd,jrf->jdf', x_in, gate_delta.reshape(rows_shape), preferre...  7.91 us
  transfers between devices with their start and end apart: 7, of which 5 were waited for; matrix products, arithmetic and copies ran while one was open for 30% of the time, Pallas kernels for 0%

commit v1 on v0

--- a/solution.py
+++ b/solution.py
@@ -95,12 +95,17 @@
     back_part = jnp.einsum(
         "jrd,jfd->jrf", dy_in, down_weight, preferred_element_type=jnp.float32
     ).astype(jnp.bfloat16)
-    back_sums = lax.psum_scatter(
-        back_part.reshape(row_count, hidden_units), "dp", scatter_dimension=0, tiled=True
+    dp_count = lax.axis_size("dp")
+    back_blocks = lax.all_to_all(
+        back_part.reshape(row_count, hidden_units), "dp", split_axis=0, concat_axis=0, tiled=True
+    )
+    back_sums = jnp.sum(
+        back_blocks.reshape(dp_count, row_count // dp_count, hidden_units).astype(jnp.float32),
+        axis=0,
     )
     front_sums = front_sums.astype(jnp.float32)
     hidden, gate_delta, up_delta = swiglu_parts(
-        front_sums[:, :hidden_units], front_sums[:, hidden_units:], back_sums.astype(jnp.float32)
+        front_sums[:, :hidden_units], front_sums[:, hidden_units:], back_sums
     )
     first = lax.all_gather(
         jnp.concatenate([hidden, gate_delta], axis=1), "dp", axis=0, tiled=True
@@ -123,9 +128,11 @@
     down_grad = jnp.einsum(
         "jrf,jrd->jfd", hidden.reshape(rows_shape), dy_in, preferred_element_type=jnp.float32
     ).astype(jnp.bfloat16)
-    gate_back = jnp.einsum(
-        "jscf,jdf->sjcd", gate_delta.reshape(expert_shape), gate_weight,
-        preferred_element_type=jnp.float32,
+    gate_back = lax.optimization_barrier(
+        jnp.einsum(
+            "jscf,jdf->sjcd", gate_delta.reshape(expert_shape), gate_weight,
+            preferred_element_type=jnp.float32,
+        )
     )
     gate_grad = jnp.einsum(
         "jrd,jrf->jdf", x_in, gate_delta.reshape(rows_shape), preferred_element_type=jnp.float32

time: 289 us -> 282 us (0.976)
  waiting for transfers between devices: 145 us -> 77.7 us
  blocking collectives: 0 us -> 58.9 us
  matrix products: 65.1 us -> 68 us
    all_to_all x0 -> x1, blocking collectives: none -> 58.9 us  [local(): lax.all_to_all(back_part.reshape(row_count, hidden_units), 'dp', split_ax...]
    reduce_scatter x1, waiting for transfers between devices: 34.4 us -> 0.02 us  [local(): front_sums = lax.psum_scatter(front, 'dp', scatter_dimension=0, tiled=True)]
    reduce_scatter x1 -> x0, waiting for transfers between devices: 30.4 us -> none  [local(): lax.psum_scatter(back_part.reshape(row_count, hidden_units), 'dp', scatte...]
    all_gather x1, waiting for transfers between devices: 3.42 us -> 0.01 us  [local(): up_delta = lax.all_gather(up_delta, 'dp', axis=0, tiled=True)]
    unnamed x26 -> x22, local copies, waits for them, and re-layouts: 7.28 us -> 7.47 us
  transfers between devices with their start and end apart: 7 -> 6, of which waited for: 5 -> 2; matrix products, arithmetic and copies ran while one was open for 30% -> 31% of each run, Pallas kernels for 0% -> 0%
where the time goes in v1:
time: 282 us; the launch traced here: 281 us
  waiting for transfers between devices  77.7 us (28%)
  matrix products  68 us (24%)
  blocking collectives  58.9 us (21%)
  local copies, waits for them, and re-layouts  35.9 us (13%)
  other arithmetic  17.6 us (6%)
  between operations  14.1 us (5%)
  starting transfers between devices  8.7 us (3%)
    all_to_all x1, blocking collectives, local(): lax.all_to_all(back_part.reshape(row_count, hidden_units), 'dp', split_ax...  58.9 us
    all_gather x1, waiting for transfers between devices, local(): lax.all_gather(jnp.concatenate([hidden, gate_delta], axis=1), 'dp', axis=...  48.7 us
    all_gather x1, waiting for transfers between devices, local(): gathered = lax.all_gather(packed, 'expert', axis=0, tiled=True)  28.8 us
    dot_general x1, matrix products, local(): jnp.einsum('jscf,jdf->sjcd', up_delta.reshape(expert_shape), up_weight, p...  11.7 us
    dot_general x1, matrix products, local(): jnp.einsum('jscf,jdf->sjcd', gate_delta.reshape(expert_shape), gate_weigh...  11.3 us
    dot_general x1, matrix products, local(): jnp.einsum('jrd,jfd->jrf', dy_in, down_weight, preferred_element_type=jnp...  9.58 us
    dot_general x1, matrix products, local(): jnp.einsum('jrd,jrf->jdf', x_in, gate_delta.reshape(rows_shape), preferre...  7.91 us
    dot_general x1, matrix products, local(): jnp.einsum('jrd,jrf->jdf', x_in, up_delta.reshape(rows_shape), preferred_...  7.89 us
  transfers between devices with their start and end apart: 6, of which 2 were waited for; matrix products, arithmetic and copies ran while one was open for 31% of the time, Pallas kernels for 0%

profile of v1, /device:TPU:0, one launch (start us, length us, event | category | flops | bytes accessed | tf_op | source)
XLA Modules:
  0.0 280.9 jit_solution(15566402002491614992)
XLA Ops:
  9.1 1.7 concatenate.9
  10.9 28.8 %all-gather.4.cloned.1.call-done = bf16[384,2176]{1,0:T(8,128)(2,1)} async-done(((bf16[48,2176]{1,0:T(8,128)(2,1)}), bf16[384,2176]{1,0:T(8,128)(2,1)}) %all-gather.4.cloned.1.call-update) | async-done | bytes 1671184 | tf_op jit(solution)/shard_map/all_gather | solution.py:52
  41.5 1.6 convert_reduce_fusion
  44.4 1.8 fusion.15
  46.5 2.9 %copy-done.2 = f32[768,2048]{1,0:T(8,128)} copy-done((f32[768,2048]{1,0:T(8,128)}, f32[768,2048]{1,0:T(8,128)S(1)}, u32[]{:S(2)}) %copy-start.2) | copy-done | bytes 6291480
  49.5 1.8 copy-done
  51.3 2.0 convolution_convert_fusion.3
  53.3 2.5 copy-done.1
  55.9 2.0 convolution_convert_fusion.4
  57.9 1.6 pad_maximum_fusion
  61.1 2.1 fusion.7
  63.2 9.6 %convolution_convert_fusion.5 = bf16[8,96,768]{2,1,0:T(8,128)(2,1)S(1)} fusion(bf16[8,96,1024]{2,1,0:T(8,128)(2,1)S(1)} %bitcast.68, bf16[8,768,1024]{2,1,0:T(8,128)(2,1)} %param.15), kind=kOutput, calls=%fused_computation.29 | convolution fusion | flops 1208549376 | bytes 15335424 | tf_op jit(solution)/shard_map/jrd,jfd->jrf/dot_general | solution.py:95
  72.8 58.9 %all_to_all.33 = bf16[4,192,768]{2,1,0:T(8,128)(2,1)S(1)} all-to-all(bf16[4,192,768]{2,1,0:T(8,128)(2,1)S(1)} %bitcast.75), channel_id=1, replica_groups=mesh['dp'=4,'expert'=8] {'dp'}, dimensions={0} | all-to-all | bytes 2359296 | tf_op jit(solution)/shard_map/all_to_all | solution.py:99
  136.1 48.7 %all-gather.6.cloned.1.call-done = bf16[768,1536]{1,0:T(8,128)(2,1)} async-done(((bf16[192,1536]{1,0:T(8,128)(2,1)}), bf16[768,1536]{1,0:T(8,128)(2,1)}) %all-gather.6.cloned.1.call-update) | async-done | bytes 2359312 | tf_op jit(solution)/shard_map/all_gather | solution.py:110
  184.8 2.8 fusion.25
  187.7 1.5 reshape.136
  189.1 3.1 %reshape.135 = bf16[8,8,12,768]{3,2,1,0:T(8,128)(2,1)} reshape(bf16[768,768]{1,0:T(8,128)(2,1)} %get-tuple-element.13) | data formatting | bytes 2359296 | tf_op jit(solution)/shard_map/reshape | solution.py:122
  192.3 7.1 %convert_bitcast_fusion = bf16[8,8,12,1024]{3,2,0,1:T(8,128)(2,1)S(1)} fusion(bf16[8,8,12,768]{3,2,1,0:T(8,128)(2,1)} %reshape.135, bf16[8,768,1024]{2,1,0:T(8,128)(2,1)} %param.15), kind=kOutput, calls=%fused_computation.23 | convolution fusion | flops 1208745984 | bytes 15335424 | tf_op jit(solution)/shard_map/jscf,jfd->sjcd/dot_general | solution.py:121
  200.3 2.0 copy.63
  202.3 3.8 %all-to-all-start.1 = ((bf16[8,96,1024]{2,1,0:T(8,128)(2,1)}), bf16[8,96,1024]{2,1,0:T(8,128)(2,1)S(1)}, u32[]{:S(2)}, u32[]{:S(2)}) async-start(bf16[8,96,1024]{2,1,0:T(8,128)(2,1)} %copy.63), calls=%async_computation.2 | async-start | bytes 3145728 | tf_op jit(solution)/shard_map/all_to_all | solution.py:125
  206.2 11.3 %fusion.8 = f32[8,8,12,1024]{3,2,0,1:T(8,128)} fusion(bf16[8,8,12,768]{3,2,1,0:T(8,128)(2,1)} %reshape.136, bf16[8,1024,768]{2,1,0:T(8,128)(2,1)} %param.13), kind=kOutput, calls=%fused_computation.22 | convolution fusion | flops 1207959552 | bytes 16908288 | tf_op jit(solution)/shard_map/jscf,jdf->sjcd/dot_general | solution.py:132
  217.5 6.6 %convolution_convert_fusion = bf16[8,768,1024]{2,1,0:T(8,128)(2,1)} fusion(bf16[8,96,768]{2,1,0:T(8,128)(2,1)S(1)} %bitcast.71, bf16[8,96,1024]{2,1,0:T(8,128)(2,1)S(1)} %bitcast.69), kind=kOutput, calls=%fused_computation.11 | convolution fusion | flops 1214251008 | bytes 15335424 | tf_op jit(solution)/shard_map/jrf,jrd->jfd/dot_general | solution.py:128
  224.1 3.1 %reshape.137 = bf16[8,8,12,768]{3,2,1,0:T(8,128)(2,1)} reshape(bf16[768,768]{1,0:T(8,128)(2,1)} %all-gather.8.cloned.1.call-done) | data formatting | bytes 2359296 | tf_op jit(solution)/shard_map/reshape | solution.py:143
  227.3 11.7 %fusion.6 = bf16[8,8,12,1024]{3,2,0,1:T(8,128)(2,1)} fusion(f32[8,8,12,1024]{3,2,0,1:T(8,128)} %fusion.8, bf16[8,8,12,768]{3,2,1,0:T(8,128)(2,1)} %reshape.137, bf16[8,1024,768]{2,1,0:T(8,128)(2,1)} %param.14), kind=kOutput, calls=%fused_computation.16 | convolution fusion | flops 1209532416 | bytes 18481152 | tf_op jit(solution)/shard_map/jscf,jdf->sjcd/dot_general | solution.py:142
  238.9 2.5 copy.67
  241.4 2.0 copy.68
  243.4 4.6 %all-to-all-start.2 = ((bf16[8,96,1024]{2,1,0:T(8,128)(2,1)}), bf16[8,96,1024]{2,1,0:T(8,128)(2,1)}, u32[]{:S(2)}, u32[]{:S(2)}) async-start(bf16[8,96,1024]{2,1,0:T(8,128)(2,1)} %copy.68), calls=%async_computation.3 | async-start | bytes 3145728 | tf_op jit(solution)/shard_map/all_to_all | solution.py:147
  248.0 7.9 %convolution_convert_fusion.2 = bf16[8,1024,768]{2,1,0:T(8,128)(2,1)} fusion(bf16[8,96,1024]{2,1,0:T(8,128)(2,1)S(1)} %bitcast.65, bf16[8,96,768]{2,1,0:T(8,128)(2,1)} %bitcast.70), kind=kOutput, calls=%fused_computation.13 | convolution fusion | flops 1214251008 | bytes 15335424 | tf_op jit(solution)/shard_map/jrd,jrf->jdf/dot_general | solution.py:137
  255.9 2.7 gather_fusion
  258.6 2.4 multiply_reduce_fusion
  261.0 7.9 %convolution_convert_fusion.1 = bf16[8,1024,768]{2,1,0:T(8,128)(2,1)} fusion(bf16[8,96,1024]{2,1,0:T(8,128)(2,1)S(1)} %bitcast.66, bf16[8,96,768]{2,1,0:T(8,128)(2,1)} %bitcast.76), kind=kOutput, calls=%fused_computation.12 | convolution fusion | flops 1214251008 | bytes 15335424 | tf_op jit(solution)/shard_map/jrd,jrf->jdf/dot_general | solution.py:150
  268.9 4.4 %gather_fusion.1 = bf16[384,1024]{1,0:T(8,128)(2,1)S(1)} fusion(bf16[768,1024]{1,0:T(8,128)(2,1)} %bitcast.17, s32[1024]{0:T(1024)S(1)} %pad_clamp_fusion), kind=kCustom, calls=%fused_computation.1.clone | custom fusion | bytes 1574400 | tf_op jit(solution)/shard_map/jit(_take)/gather | solution.py:162
  (70 shorter events, 13.1 us)
Async XLA Ops:
  7.2 32.6 %all-gather.4.cloned.1.call-start = ((), (), s32[]{:S(2)}) async-start(), calls=%async_computation.4 | async-start | bytes 1880064 | tf_op jit(solution)/shard_map/all_gather | solution.py:52
  10.8 121.2 %reduce-scatter.2.cloned.1.call-start = ((), (), s32[]{:S(2)}) async-start(), calls=%async_computation.5 | async-start | bytes 2949120 | tf_op jit(solution)/shard_map/reduce_scatter | solution.py:94
  39.8 4.7 %copy-start.7 = (bf16[384,2176]{1,0:T(8,128)(2,1)S(1)}, bf16[384,2176]{1,0:T(8,128)(2,1)}, u32[]{:S(2)}) copy-start(bf16[384,2176]{1,0:T(8,128)(2,1)} %all-gather.4.cloned.1.call-done) | copy-start | bytes 5013508
  44.4 6.9 %copy-start = (bf16[8,1024,768]{2,1,0:T(8,128)(2,1)S(1)}, bf16[8,1024,768]{2,1,0:T(8,128)(2,1)}, u32[]{:S(2)}) copy-start(bf16[8,1024,768]{2,1,0:T(8,128)(2,1)} %param.14) | copy-start | bytes 37748740
  46.3 3.2 %copy-start.2 = (f32[768,2048]{1,0:T(8,128)}, f32[768,2048]{1,0:T(8,128)S(1)}, u32[]{:S(2)}) copy-start(f32[768,2048]{1,0:T(8,128)S(1)} %fusion.15) | copy-start | bytes 18874372
  51.3 4.6 %copy-start.1 = (bf16[8,1024,768]{2,1,0:T(8,128)(2,1)S(1)}, bf16[8,1024,768]{2,1,0:T(8,128)(2,1)}, u32[]{:S(2)}) copy-start(bf16[8,1024,768]{2,1,0:T(8,128)(2,1)} %param.13) | copy-start | bytes 37748740
  59.5 125.3 %all-gather.6.cloned.1.call-start = ((), (), s32[]{:S(2)}) async-start(), calls=%async_computation.6 | async-start | bytes 2949120 | tf_op jit(solution)/shard_map/all_gather | solution.py:110
  63.2 9.6 %copy-start.3 = (bf16[768,1024]{1,0:T(8,128)(2,1)}, bf16[768,1024]{1,0:T(8,128)(2,1)S(1)}, u32[]{:S(2)}) copy-start(bf16[768,1024]{1,0:T(8,128)(2,1)S(1)} %fusion.7) | copy-start | bytes 4718596
  133.2 2.0 copy-start.9
  133.2 2.1 copy-start.8
  135.1 89.0 %all-gather.8.cloned.1.call-start = ((), (), s32[]{:S(2)}) async-start(), calls=%async_computation.7 | async-start | bytes 1474560 | tf_op jit(solution)/shard_map/all_gather | solution.py:114
  187.6 4.6 %copy-start.5 = (bf16[768,768]{1,0:T(8,128)(2,1)}, bf16[768,768]{1,0:T(8,128)(2,1)S(1)}, u32[]{:S(2)}) copy-start(bf16[768,768]{1,0:T(8,128)(2,1)S(1)} %get-tuple-element.12) | copy-start | bytes 3538948
  202.3 41.1 %all-to-all-start.1 = ((bf16[8,96,1024]{2,1,0:T(8,128)(2,1)}), bf16[8,96,1024]{2,1,0:T(8,128)(2,1)S(1)}, u32[]{:S(2)}, u32[]{:S(2)}) async-start(bf16[8,96,1024]{2,1,0:T(8,128)(2,1)} %copy.63), calls=%async_computation.2 | async-start | bytes 3145728 | tf_op jit(solution)/shard_map/all_to_all | solution.py:125
  206.2 11.4 %copy-start.4 = (bf16[768,1024]{1,0:T(8,128)(2,1)S(1)}, bf16[768,1024]{1,0:T(8,128)(2,1)}, u32[]{:S(2)}) copy-start(bf16[768,1024]{1,0:T(8,128)(2,1)} %copy-done.3) | copy-start | bytes 4718596
  206.2 11.4 %copy-start.6 = (bf16[768,768]{1,0:T(8,128)(2,1)S(1)}, bf16[768,768]{1,0:T(8,128)(2,1)}, u32[]{:S(2)}) copy-start(bf16[768,768]{1,0:T(8,128)(2,1)} %get-tuple-element.13) | copy-start | bytes 3538948
  243.4 25.5 %all-to-all-start.2 = ((bf16[8,96,1024]{2,1,0:T(8,128)(2,1)}), bf16[8,96,1024]{2,1,0:T(8,128)(2,1)}, u32[]{:S(2)}, u32[]{:S(2)}) async-start(bf16[8,96,1024]{2,1,0:T(8,128)(2,1)} %copy.68), calls=%async_computation.3 | async-start | bytes 3145728 | tf_op jit(solution)/shard_map/all_to_all | solution.py:147
Sparse Core Ops, SparseCore 0:
  10.9 28.7 all-gather.3
  59.6 66.6 reduce-scatter.1
  135.2 49.5 all-gather.5
  187.8 29.2 all-gather.7
